TPU v7x, 128 devices: a whole 4x4x4 slice. The times are simulated.
128 devices in a mesh: req: 4 (over y), head: 8 (over z, x_hi), blk: 4 (over x_lo, core).
Axes of the slice: x: 4 (x_hi: 2, x_lo: 2; x = x_hi * 2 + x_lo), y: 4, z: 4, core: 2. Of those that a mesh axis runs over, the one named last changes fastest.
Arguments:
- image_hidden: bfloat16 [16, 32, 32, 1536], P('req', 'head', 'blk'), parts along dimension 0, may hold values from -6 to 6
- text_hidden: bfloat16 [16, 160, 1536], P('req', ('head', 'blk')), parts along dimension 0, may hold values from -6 to 6
- latent_grid: float32 [16, 64, 64, 16], P('req', 'head', 'blk'), parts along dimension 0, may hold values from -6 to 6
- text_lengths: int32 [16], P('req'), parts along dimension 0, may hold values from 38 to 154, as said below
- step_index: int32 [16], P('req'), parts along dimension 0, may hold values from 125 to 999
- image_mod: float32 [16, 6, 1536], P('req'), parts along dimension 0, may hold values from -3 to 3
- text_mod: float32 [16, 6, 1536], P('req'), parts along dimension 0, may hold values from -3 to 3
- final_mod: float32 [16, 2, 1536], P('req'), parts along dimension 0, may hold values from -3 to 3
- image_qk_gain: float32 [2, 64], replicated, may hold values from 0.5 to 2.3
- text_qk_gain: float32 [2, 64], replicated, may hold values from 0.5 to 2.3
- image_qkv: bfloat16 [1536, 3, 1536], P(None, None, 'head'), may hold values from -0.15625 to 0.15625
- text_qkv: bfloat16 [1536, 3, 1536], P(None, None, 'head'), may hold values from -0.15625 to 0.15625
- image_proj: bfloat16 [1536, 1536], P('head'), may hold values from -0.15625 to 0.15625
- text_proj: bfloat16 [1536, 1536], P('head'), may hold values from -0.15625 to 0.15625
- image_up: bfloat16 [1536, 6144], P(None, 'head'), may hold values from -0.15625 to 0.15625
- text_up: bfloat16 [1536, 6144], P(None, 'head'), may hold values from -0.15625 to 0.15625
- image_down: bfloat16 [6144, 1536], P('head'), may hold values from -0.078125 to 0.078125
- text_down: bfloat16 [6144, 1536], P('head'), may hold values from -0.078125 to 0.078125
- final_proj: bfloat16 [1536, 64], replicated, may hold values from -0.15625 to 0.15625
- conv_kernel: bfloat16 [3, 3, 16, 512], replicated, may hold values from -0.5 to 0.5
Outputs:
- image_states: bfloat16 [16, 32, 32, 1536], P('req', 'head', 'blk'), parts along dimension 0
- text_states: bfloat16 [16, 160, 1536], P('req', ('head', 'blk')), parts along dimension 0
- latent_next: float32 [16, 64, 64, 16], P('req', 'head', 'blk'), parts along dimension 0
- features: bfloat16 [16, 64, 64, 512], P('req', 'head', 'blk'), parts along dimension 0
There are 4 independent parts, one for each index of `req`. A program takes and returns all parts, laid end to end along the dimension named above; an argument that names none is the same for every part. Nothing has to cross between parts.
Inputs may be any that keep to these rules, and one draw needn't show every extreme that they name: `text_lengths`: every request has 154 or fewer live text tokens, and in each group one request has exactly 154.
All inputs are finite; a program needn't handle non-finite values.
Results may differ from a plain program's by a relative error of at most 0.012.
Values may be sent and summed in bfloat16 or wider, within the bound.
No kernel may reach another device: no remote copies, remote signals or barrier semaphores. Data moves between devices by JAX's collectives and lax.ppermute only.
A program may use at most 128 MiB of HBM per device.

v0:
```python
import math
import jax
import jax.numpy as jnp
from jax import lax
from jax.sharding import PartitionSpec as P

HD = 64


def extended(block, sides, width):
    for axis, dim in sides:
        count = lax.axis_size(axis)
        forward = [(i, i + 1) for i in range(count - 1)]
        backward = [(target, source) for source, target in forward]
        low = lax.ppermute(
            lax.slice_in_dim(block, block.shape[dim] - width, None, axis=dim), axis, forward
        )
        high = lax.ppermute(lax.slice_in_dim(block, 0, width, axis=dim), axis, backward)
        block = jnp.concatenate([low, block, high], axis=dim)
    return block


def expand(vector, values):
    return vector.reshape((vector.shape[0],) + (1,) * (values.ndim - 2) + (vector.shape[-1],))


def modulate(values, shift, scale):
    average = jnp.mean(values, -1, keepdims=True)
    centred = values - average
    spread = jnp.mean(centred * centred, -1, keepdims=True)
    normed = centred * lax.rsqrt(spread + 1e-06)
    return normed * (1.0 + expand(scale, values)) + expand(shift, values)


def head_norm(values, gain):
    shaped = values.reshape(values.shape[:-1] + (values.shape[-1] // HD, HD))
    return (shaped * lax.rsqrt(jnp.mean(shaped * shaped, -1, keepdims=True) + 1e-06) * gain).astype(
        jnp.bfloat16
    )


def noise_level(fraction):
    return 3.0 * fraction / (1.0 + 2.0 * fraction)


def attention_inputs(normed, weight, gains):
    projected = jnp.einsum("rnd,dje->rnje", normed, weight, preferred_element_type=jnp.float32)
    queries = head_norm(projected[:, :, 0], gains[0])
    key_heads = head_norm(projected[:, :, 1], gains[1])
    value_heads = projected[:, :, 2].reshape(queries.shape).astype(jnp.bfloat16)
    return (queries, key_heads, value_heads)


def convolve(padded, kernel):
    out_rows = padded.shape[1] - 2
    out_cols = padded.shape[2] - 2
    summed = jnp.zeros((padded.shape[0], out_rows, out_cols, kernel.shape[-1]), jnp.float32)
    for row_off in range(3):
        for col_off in range(3):
            summed = summed + jnp.einsum(
                "rhwc,co->rhwo",
                padded[:, row_off : row_off + out_rows, col_off : col_off + out_cols],
                kernel[row_off, col_off],
                preferred_element_type=jnp.float32,
            )
    return summed.astype(jnp.bfloat16)


def body(
    image_hidden,
    text_hidden,
    latent_grid,
    text_lengths,
    step_index,
    image_mod,
    text_mod,
    final_mod,
    image_qk_gain,
    text_qk_gain,
    image_qkv,
    text_qkv,
    image_proj,
    text_proj,
    image_up,
    text_up,
    image_down,
    text_down,
    final_proj,
    conv_kernel,
):
    blocks = lax.axis_size("blk")
    requests, tile_rows, tile_cols, model_width = image_hidden.shape
    text_slice = text_hidden.shape[1]
    image_full, text_full = (
        lax.all_gather(image_hidden, "head", axis=1, tiled=True),
        lax.all_gather(text_hidden, "head", axis=1, tiled=True),
    )
    grid_rows = image_full.shape[1]
    image_rows = grid_rows * tile_cols
    text_rows = text_full.shape[1]
    local_rows = image_rows + text_rows
    image_flat = image_full.reshape(requests, image_rows, model_width).astype(jnp.float32)
    text_flat = text_full.astype(jnp.float32)
    image_norm = modulate(image_flat, image_mod[:, 0], image_mod[:, 1]).astype(jnp.bfloat16)
    text_norm = modulate(text_flat, text_mod[:, 0], text_mod[:, 1]).astype(jnp.bfloat16)
    image_q, image_k, image_v = attention_inputs(image_norm, image_qkv, image_qk_gain)
    text_q, text_k, text_v = attention_inputs(text_norm, text_qkv, text_qk_gain)
    queries = jnp.concatenate([image_q, text_q], 1)
    key_heads = jnp.concatenate([image_k, text_k], 1)
    value_heads = jnp.concatenate([image_v, text_v], 1)
    local_heads = queries.shape[2]
    score_scale = 1.0 / math.sqrt(HD)
    key_piece = lax.all_gather(key_heads, "blk", axis=1, tiled=True)
    value_piece = lax.all_gather(value_heads, "blk", axis=1, tiled=True)
    span_rows = key_piece.shape[1]
    position = jnp.arange(span_rows, dtype=jnp.int32)
    source = position // local_rows
    within = position % local_rows
    text_pos = within - image_rows
    owner = text_pos // text_slice
    slot_ids = (owner * blocks + source) * text_slice + text_pos % text_slice
    usable = (within < image_rows)[None, :] | (slot_ids[None, :] < text_lengths[:, None])
    scores = (
        jnp.einsum("rqhd,rkhd->rhqk", queries, key_piece, preferred_element_type=jnp.float32)
        * score_scale
    )
    weights = jnp.exp(scores) * usable[:, None, None, :].astype(jnp.float32)
    denominator = jnp.sum(weights, -1)
    numerator = jnp.einsum(
        "rhqk,rkhd->rhqd",
        weights.astype(jnp.bfloat16),
        value_piece,
        preferred_element_type=jnp.float32,
    )
    numerator, denominator = (numerator, denominator)
    context = (numerator / denominator[..., None]).astype(jnp.bfloat16)
    local_width = local_heads * HD
    context = context.transpose(0, 2, 1, 3).reshape(requests, local_rows, local_width)
    image_part = jnp.einsum(
        "rne,ed->rnd", context[:, :image_rows], image_proj, preferred_element_type=jnp.float32
    )
    text_part = jnp.einsum(
        "rne,ed->rnd", context[:, image_rows:], text_proj, preferred_element_type=jnp.float32
    )
    image_attn, text_attn = (
        lax.psum_scatter(
            image_part.reshape(requests, grid_rows, tile_cols, model_width).astype(jnp.bfloat16),
            "head",
            scatter_dimension=1,
            tiled=True,
        ).astype(jnp.float32),
        lax.psum_scatter(
            text_part.astype(jnp.bfloat16), "head", scatter_dimension=1, tiled=True
        ).astype(jnp.float32),
    )
    image_mid = image_hidden.astype(jnp.float32) + expand(image_mod[:, 2], image_attn) * image_attn
    text_mid = text_hidden.astype(jnp.float32) + expand(text_mod[:, 2], text_attn) * text_attn
    image_local = modulate(image_mid, image_mod[:, 3], image_mod[:, 4]).astype(jnp.bfloat16)
    text_local = modulate(text_mid, text_mod[:, 3], text_mod[:, 4]).astype(jnp.bfloat16)
    image_in, text_in = (
        lax.all_gather(image_local, "head", axis=1, tiled=True),
        lax.all_gather(text_local, "head", axis=1, tiled=True),
    )
    image_in = image_in.reshape(requests, image_rows, model_width)
    image_hid = jax.nn.gelu(
        jnp.einsum("rnd,df->rnf", image_in, image_up, preferred_element_type=jnp.float32),
        approximate=True,
    ).astype(jnp.bfloat16)
    text_hid = jax.nn.gelu(
        jnp.einsum("rnd,df->rnf", text_in, text_up, preferred_element_type=jnp.float32),
        approximate=True,
    ).astype(jnp.bfloat16)
    image_back = jnp.einsum(
        "rnf,fd->rnd", image_hid, image_down, preferred_element_type=jnp.float32
    ).reshape(requests, grid_rows, tile_cols, model_width)
    text_back = jnp.einsum("rnf,fd->rnd", text_hid, text_down, preferred_element_type=jnp.float32)
    image_mlp, text_mlp = (
        lax.psum_scatter(
            image_back.astype(jnp.bfloat16), "head", scatter_dimension=1, tiled=True
        ).astype(jnp.float32),
        lax.psum_scatter(
            text_back.astype(jnp.bfloat16), "head", scatter_dimension=1, tiled=True
        ).astype(jnp.float32),
    )
    image_out = image_mid + expand(image_mod[:, 5], image_mlp) * image_mlp
    image_states = image_out.astype(jnp.bfloat16)
    text_states = (text_mid + expand(text_mod[:, 5], text_mlp) * text_mlp).astype(jnp.bfloat16)
    final_in = modulate(image_out, final_mod[:, 1], final_mod[:, 0]).astype(jnp.bfloat16)
    velocity = jnp.einsum("rhwd,dp->rhwp", final_in, final_proj, preferred_element_type=jnp.float32)
    channels = velocity.shape[-1] // 4
    velocity = (
        velocity.reshape(requests, tile_rows, tile_cols, 2, 2, channels)
        .transpose(0, 1, 3, 2, 4, 5)
        .reshape(requests, 2 * tile_rows, 2 * tile_cols, channels)
    )
    current = step_index.astype(jnp.float32) / 1000.0
    following = jnp.maximum(step_index - 125, 0).astype(jnp.float32) / 1000.0
    step_size = noise_level(following) - noise_level(current)
    latent_next = latent_grid + step_size[:, None, None, None] * velocity
    decoded_in = (latent_next / 1.5305 + 0.0609).astype(jnp.bfloat16)
    padded = extended(decoded_in, (("head", 1), ("blk", 2)), 1)
    features = convolve(padded, conv_kernel)
    return (image_states, text_states, latent_next, features)


def solution(mesh):
    in_specs = (
        P("req", "head", "blk", None),
        P("req", ("head", "blk"), None),
        P("req", "head", "blk", None),
        P("req"),
        P("req"),
        P("req", None, None),
        P("req", None, None),
        P("req", None, None),
        P(),
        P(),
        P(None, None, "head"),
        P(None, None, "head"),
        P("head", None),
        P("head", None),
        P(None, "head"),
        P(None, "head"),
        P("head", None),
        P("head", None),
        P(),
        P(),
    )
    out_specs = (
        P("req", "head", "blk", None),
        P("req", ("head", "blk"), None),
        P("req", "head", "blk", None),
        P("req", "head", "blk", None),
    )
    return jax.shard_map(body, mesh=mesh, in_specs=in_specs, out_specs=out_specs, check_vma=False)
```

profile of v0, /device:TPU:1, one launch (start us, length us, event | category | flops | bytes accessed | tf_op | source)
XLA Modules:
  0.0 633.5 jit_solution(10010168062454504127)
XLA Ops:
  8.0 1.6 slice_bitcast_fusion.4
  11.7 33.0 %all_gather.19 = bf16[4,40,1536]{2,0,1:T(4,128)(2,1)S(1)} all-gather(bf16[4,5,1536]{2,0,1:T(4,128)(2,1)} %param.21), channel_id=1, replica_groups=mesh['req'=4,'head'=8,'blk'=4] {'head'}, dimensions={1}, use_global_device_ids=true | all-gather | bytes 552960 | tf_op jit(solution)/shard_map/all_gather | solution.py:96
  49.0 28.9 %all-gather.5.cloned.1.call-done = bf16[4,32,8,1536]{3,2,1,0:T(8,128)(2,1)} async-done(((bf16[4,4,8,1536]{3,2,1,0:T(8,128)(2,1)}), bf16[4,32,8,1536]{3,2,1,0:T(8,128)(2,1)}) %all-gather.5.cloned.1.call-update) | async-done | bytes 3145744 | tf_op jit(solution)/shard_map/all_gather | solution.py:95
  77.8 2.4 convert_reduce_fusion
  80.3 2.9 fusion.11
  83.3 4.6 fusion.25
  90.3 3.1 copy.76
  96.1 1.7 convert_element_type.137
  97.8 1.6 copy.79
  100.3 2.0 slice.285
  102.3 2.1 copy.78
  104.4 2.9 pad_maximum_fusion
  112.4 21.7 %all-gather.7.cloned.1.call-done = bf16[4,1184,3,64]{3,0,2,1:T(4,128)(2,1)} async-done(((bf16[4,296,3,64]{3,0,2,1:T(4,128)(2,1)}), bf16[4,1184,3,64]{3,0,2,1:T(4,128)(2,1)}) %all-gather.7.cloned.1.call-update) | async-done | bytes 1818640 | tf_op jit(solution)/shard_map/all_gather | solution.py:113
  134.1 10.5 %fusion = (f32[4,3,296]{2,1,0:T(4,128)S(1)}, f32[4,3,296,1184]{3,2,1,0:T(8,128)}) fusion(f32[4,1184]{1,0:T(4,128)S(1)} %or_convert_fusion, bf16[4,1184,3,64]{3,0,2,1:T(4,128)(2,1)} %all-gather.7.cloned.1.call-done, bf16[4,40,3,64]{1,3,2,0:T(8,128)(2,1)S(1)} %multiply_convert_fusion.3, bf16[4,256,3,64]{1,3,2,0:T(8,128)(2,1)} %multiply_convert_fusion.1), kind=kOutput, calls=%fused_computation.2 | convolution fusion | flops 551835136 | bytes 19128704 | tf_op jit(solution)/shard_map/rqhd,rkhd->rhqk/dot_general | solution.py:124
  144.6 34.0 %all-gather.9.cloned.1.call-done = bf16[4,1184,3,64]{3,0,2,1:T(4,128)(2,1)} async-done(((bf16[4,296,3,64]{3,0,2,1:T(4,128)(2,1)}), bf16[4,1184,3,64]{3,0,2,1:T(4,128)(2,1)}) %all-gather.9.cloned.1.call-update) | async-done | bytes 1818640 | tf_op jit(solution)/shard_map/all_gather | solution.py:114
  178.5 9.1 %divide_convert_fusion = bf16[4,296,3,64]{1,3,2,0:T(8,128)(2,1)S(1)} fusion(bf16[4,1184,3,64]{3,0,2,1:T(4,128)(2,1)} %all-gather.9.cloned.1.call-done, f32[4,3,296,1184]{3,2,1,0:T(8,128)} %get-tuple-element.49, f32[4,1184]{1,0:T(4,128)S(1)} %or_convert_fusion, f32[4,296,3]{1,2,0:T(4,128)S(1)} %bitcast.223), kind=kOutput, calls=%fused_computation.61 | convolution fusion | flops 547178496 | bytes 19128704 | tf_op jit(solution)/shard_map/rhqk,rkhd->rhqd/dot_general | solution.py:129
  187.6 2.7 fusion.15
  193.2 164.2 %all-reduce.11.cloned.1.call-done = (bf16[4,32,8,1536]{3,2,1,0:T(8,128)(2,1)}, bf16[4,40,1536]{2,0,1:T(4,128)(2,1)}) async-done(((bf16[4,32,8,1536]{3,2,1,0:T(8,128)(2,1)}, bf16[4,40,1536]{2,0,1:T(4,128)(2,1)}), (bf16[4,32,8,1536]{3,2,1,0:T(8,128)(2,1)}, bf16[4,40,1536]{2,0,1:T(4,128)(2,1)})) %all-reduce.11.cloned.1.call-update) | async-done | bytes 3637264
  359.9 2.1 add_convert_fusion.1
  365.7 30.7 %all_gather.23 = bf16[4,40,1536]{2,0,1:T(4,128)(2,1)S(1)} all-gather(bf16[4,5,1536]{2,0,1:T(4,128)(2,1)S(1)} %add_convert_fusion.5), channel_id=1, replica_groups=mesh['req'=4,'head'=8,'blk'=4] {'head'}, dimensions={1}, use_global_device_ids=true | all-gather | bytes 552960 | tf_op jit(solution)/shard_map/all_gather | solution.py:162
  396.4 4.8 convolution_convert_fusion.2
  401.2 2.1 copy.86
  403.3 23.0 %all-gather.11.cloned.1.call-done = bf16[4,32,8,1536]{3,2,1,0:T(8,128)(2,1)} async-done(((bf16[4,4,8,1536]{3,2,1,0:T(8,128)(2,1)}), bf16[4,32,8,1536]{3,2,1,0:T(8,128)(2,1)}) %all-gather.11.cloned.1.call-update) | async-done | bytes 3145744 | tf_op jit(solution)/shard_map/all_gather | solution.py:161
  426.2 10.5 %fusion.14 = bf16[4,32,8,1536]{3,2,1,0:T(8,128)(2,1)} fusion(bf16[768,1536]{1,0:T(8,128)(2,1)S(1)} %copy-done, bf16[1536,768]{1,0:T(8,128)(2,1)} %param.34, bf16[4,32,8,1536]{3,2,1,0:T(8,128)(2,1)} %all-gather.11.cloned.1.call-done), kind=kOutput, calls=%fused_computation.21 | convolution fusion | flops 4840488960 | bytes 11010048 | tf_op jit(solution)/shard_map/rnf,fd->rnd/dot_general | solution.py:173
  437.6 161.8 %all-reduce.9.cloned.1.call-done = (bf16[4,32,8,1536]{3,2,1,0:T(8,128)(2,1)}, bf16[4,40,1536]{2,0,1:T(4,128)(2,1)}) async-done(((bf16[4,32,8,1536]{3,2,1,0:T(8,128)(2,1)}, bf16[4,40,1536]{2,0,1:T(4,128)(2,1)}), (bf16[4,32,8,1536]{3,2,1,0:T(8,128)(2,1)}, bf16[4,40,1536]{2,0,1:T(4,128)(2,1)})) %all-reduce.9.cloned.1.call-update) | async-done | bytes 3637264
  600.8 2.2 multiply_reduce_fusion
  603.0 1.6 fusion.96
  605.8 2.0 collective-permute-start
  610.9 2.8 collective-permute-done.1
  613.8 5.1 collective-permute-start.2
  618.9 1.9 collective-permute-start.3
  621.4 2.6 collective-permute-done.3
  (139 shorter events, 35.6 us)
Async XLA Ops:
  7.2 419.1 %copy-start = (bf16[768,1536]{1,0:T(8,128)(2,1)S(1)}, bf16[768,1536]{1,0:T(8,128)(2,1)}, u32[]{:S(2)}) copy-start(bf16[768,1536]{1,0:T(8,128)(2,1)} %param.36) | copy-start | bytes 7077892
  7.2 70.7 %all-gather.5.cloned.1.call-start = ((), (), s32[]{:S(2)}) async-start(), calls=%async_computation | async-start | bytes 3538944 | tf_op jit(solution)/shard_map/all_gather | solution.py:95
  7.9 126.1 %all-gather.7.cloned.1.call-start = ((), (), s32[]{:S(2)}) async-start(), calls=%async_computation.1 | async-start | bytes 4546560 | tf_op jit(solution)/shard_map/all_gather | solution.py:113
  8.0 38.0 %copy-start.2 = (bf16[1536,3,192]{0,2,1:T(8,128)(2,1)S(1)}, bf16[1536,3,192]{0,2,1:T(8,128)(2,1)}, u32[]{:S(2)}) copy-start(bf16[1536,3,192]{0,2,1:T(8,128)(2,1)} %param.31) | copy-start | bytes 5308420
  45.4 2.8 copy-start.18
  45.4 2.8 copy-start.19
  46.7 0.8 copy-start.3
  48.9 34.4 %copy-start.16 = (f32[4,1536]{1,0:T(4,128)S(1)}, f32[4,1536]{1,0:T(4,128)}, u32[]{:S(2)}) copy-start(f32[4,1536]{1,0:T(4,128)} %get-tuple-element.36) | copy-start | bytes 73732
  48.9 34.4 %copy-start.17 = (f32[4,1,1536]{2,0,1:T(4,128)S(1)}, f32[4,1,1536]{2,0,1:T(4,128)}, u32[]{:S(2)}) copy-start(f32[4,1,1536]{2,0,1:T(4,128)} %copy.149) | copy-start | bytes 73732
  88.0 1.4 copy-start.4
  93.4 85.1 %all-gather.9.cloned.1.call-start = ((), (), s32[]{:S(2)}) async-start(), calls=%async_computation.2 | async-start | bytes 4546560 | tf_op jit(solution)/shard_map/all_gather | solution.py:114
  107.3 250.0 %all-reduce.11.cloned.1.call-start = ((), (), s32[]{:S(2)}) async-start(), calls=%async_computation.5 | async-start | bytes 7274496
  178.5 9.1 %copy-start.7 = (bf16[192,1536]{1,0:T(8,128)(2,1)S(1)}, bf16[192,1536]{1,0:T(8,128)(2,1)}, u32[]{:S(2)}) copy-start(bf16[192,1536]{1,0:T(8,128)(2,1)} %param.32) | copy-start | bytes 1769476
  187.6 2.7 copy-start.6
  190.4 1.5 copy-start.13
  190.4 1.5 copy-start.21
  190.4 167.0 %copy-start.1 = (bf16[4,4,8,1536]{3,2,1,0:T(8,128)(2,1)S(1)}, bf16[4,4,8,1536]{3,2,1,0:T(8,128)(2,1)}, u32[]{:S(2)}) copy-start(bf16[4,4,8,1536]{3,2,1,0:T(8,128)(2,1)} %param.20) | copy-start | bytes 1179652
  190.7 169.2 %copy-start.14 = (f32[4,1536]{1,0:T(4,128)S(1)}, f32[4,1536]{1,0:T(4,128)}, u32[]{:S(2)}) copy-start(f32[4,1536]{1,0:T(4,128)} %get-tuple-element.39) | copy-start | bytes 73732
  191.7 170.9 %copy-start.12 = (f32[4,1,1536]{2,0,1:T(4,128)S(1)}, f32[4,1,1536]{2,0,1:T(4,128)}, u32[]{:S(2)}) copy-start(f32[4,1,1536]{2,0,1:T(4,128)} %get-tuple-element.32) | copy-start | bytes 73732
  191.8 171.0 %copy-start.5 = (bf16[4,5,1536]{2,0,1:T(4,128)(2,1)S(1)}, bf16[4,5,1536]{2,0,1:T(4,128)(2,1)}, u32[]{:S(2)}) copy-start(bf16[4,5,1536]{2,0,1:T(4,128)(2,1)} %param.21) | copy-start | bytes 184324
  191.8 173.0 %copy-start.11 = (f32[4,1536]{1,0:T(4,128)S(1)}, f32[4,1536]{1,0:T(4,128)}, u32[]{:S(2)}) copy-start(f32[4,1536]{1,0:T(4,128)} %get-tuple-element.33) | copy-start | bytes 73732
  191.8 234.4 %all-gather.11.cloned.1.call-start = ((), (), s32[]{:S(2)}) async-start(), calls=%async_computation.3 | async-start | bytes 3538944 | tf_op jit(solution)/shard_map/all_gather | solution.py:161
  362.0 237.4 %all-reduce.9.cloned.1.call-start = ((), (), s32[]{:S(2)}) async-start(), calls=%async_computation.4 | async-start | bytes 7274496
  436.7 0.7 copy-start.20
  436.7 0.8 copy-start.15
  437.6 167.4 %copy-start.8 = (f32[4,8,16,16]{3,2,1,0:T(8,128)S(1)}, f32[4,8,16,16]{3,2,1,0:T(8,128)}, u32[]{:S(2)}) copy-start(f32[4,8,16,16]{3,2,1,0:T(8,128)} %param.22) | copy-start | bytes 98308
  600.8 8.3 %copy-start.10 = (f32[4,1536]{1,0:T(4,128)S(1)}, f32[4,1536]{1,0:T(4,128)}, u32[]{:S(2)}) copy-start(f32[4,1536]{1,0:T(4,128)} %get-tuple-element.28) | copy-start | bytes 73732
  600.8 9.9 %copy-start.9 = (bf16[3,3,16,512]{3,2,1,0:T(8,128)(2,1)S(1)}, bf16[3,3,16,512]{3,2,1,0:T(8,128)(2,1)}, u32[]{:S(2)}) copy-start(bf16[3,3,16,512]{3,2,1,0:T(8,128)(2,1)} %param.39) | copy-start | bytes 442372
  605.8 5.1 collective-permute-start
  607.8 6.0 collective-permute-start.1
  613.8 7.6 %collective-permute-start.2 = (bf16[4,10,1,16]{3,2,1,0:T(2,128)(2,1)S(1)}, bf16[4,10,1,16]{3,2,1,0:T(2,128)(2,1)S(1)}, u32[]{:S(2)}, u32[]{:S(2)}) collective-permute-start(bf16[4,10,1,16]{3,2,1,0:T(2,128)(2,1)S(1)} %get-tuple-element.26), channel_id=1, source_target_pairs={{0,1},{1,2},{2,3},{4,5},{5,6},{6,7},{8,9},{9,10},{10,11},{12,13},{... | collective-permute-start | bytes 3848 | tf_op jit(solution)/shard_map/ppermute | solution.py:15
  618.9 5.1 collective-permute-start.3
Sparse Core Ops, SparseCore 0:
  10.3 67.4 all-gather.4
  93.5 40.4 all-gather.6
  135.7 42.7 all-gather.8
  191.9 165.4 all-reduce.10
  362.1 64.0 all-gather.10
  436.9 162.4 all-reduce.8
where the time goes:
time: 635 us; the launch traced here: 633 us
  waiting for transfers between devices  440 us (69%)
  blocking collectives  63.7 us (10%)
  matrix products  48.2 us (8%)
  other arithmetic  31.5 us (5%)
  local copies, waits for them, and re-layouts  23.8 us (4%)
  between operations  16 us (3%)
  starting transfers between devices  10.7 us (2%)
    unnamed x8, waiting for transfers between devices  327 us
    all_gather x1, waiting for transfers between devices, body(): value_piece = lax.all_gather(value_heads, 'blk', axis=1, tiled=True)  34 us
    all_gather x1, blocking collectives, body(): lax.all_gather(text_hidden, 'head', axis=1, tiled=True)  33 us
    all_gather x1, blocking collectives, body(): lax.all_gather(text_local, 'head', axis=1, tiled=True)  30.7 us
    all_gather x1, waiting for transfers between devices, body(): lax.all_gather(image_hidden, 'head', axis=1, tiled=True)  28.9 us
    all_gather x1, waiting for transfers between devices, body(): lax.all_gather(image_local, 'head', axis=1, tiled=True)  23 us
    all_gather x1, waiting for transfers between devices, body(): key_piece = lax.all_gather(key_heads, 'blk', axis=1, tiled=True)  21.7 us
  transfers between devices with their start and end apart: 10, of which 8 were waited for; matrix products, arithmetic and copies ran while one was open for 8% of the time, Pallas kernels for 0%

commit v1 on v0

--- a/solution.py
+++ b/solution.py
@@ -92,7 +92,9 @@
     requests, tile_rows, tile_cols, model_width = image_hidden.shape
     text_slice = text_hidden.shape[1]
     image_full, text_full = (
-        lax.all_gather(image_hidden, "head", axis=1, tiled=True),
+        jnp.concatenate(
+            lax.all_to_all(jnp.stack([image_hidden] * lax.axis_size("head")), "head", 0, 0), axis=1
+        ),
         lax.all_gather(text_hidden, "head", axis=1, tiled=True),
     )
     grid_rows = image_full.shape[1]

time: 635 us -> 648 us (1.020)
  blocking collectives: 63.7 us -> 92.2 us
  waiting for transfers between devices: 440 us -> 416 us
  starting transfers between devices: 10.7 us -> 19.1 us
    all_gather x1 -> x0, waiting for transfers between devices: 28.9 us -> none  [body(): lax.all_gather(image_hidden, 'head', axis=1, tiled=True)]
    all_gather x1, blocking collectives: 33 us -> 61.5 us  [body(): lax.all_gather(text_hidden, 'head', axis=1, tiled=True)]
    all_to_all x0 -> x1, starting transfers between devices: none -> 8.45 us  [body(): lax.all_to_all(jnp.stack([image_hidden] * lax.axis_size('head')), 'head',...]
    unnamed x8 -> x7, waiting for transfers between devices: 327 us -> 326 us
  transfers between devices with their start and end apart: 10 -> 10, of which waited for: 8 -> 7; matrix products, arithmetic and copies ran while one was open for 8% -> 7% of each run, Pallas kernels for 0% -> 0%
where the time goes in v1:
time: 648 us; the launch traced here: 647 us
  waiting for transfers between devices  416 us (64%)
  blocking collectives  92.2 us (14%)
  matrix products  45.5 us (7%)
  other arithmetic  32.1 us (5%)
  local copies, waits for them, and re-layouts  26.4 us (4%)
  starting transfers between devices  19.1 us (3%)
  between operations  15.7 us (2%)
    unnamed x7, waiting for transfers between devices  326 us
    all_gather x1, blocking collectives, body(): lax.all_gather(text_hidden, 'head', axis=1, tiled=True)  61.5 us
    all_gather x1, waiting for transfers between devices, body(): value_piece = lax.all_gather(value_heads, 'blk', axis=1, tiled=True)  34 us
    all_gather x1, blocking collectives, body(): lax.all_gather(text_local, 'head', axis=1, tiled=True)  30.7 us
    all_gather x1, waiting for transfers between devices, body(): key_piece = lax.all_gather(key_heads, 'blk', axis=1, tiled=True)  27.2 us
    all_gather x1, waiting for transfers between devices, body(): lax.all_gather(image_local, 'head', axis=1, tiled=True)  23 us
  transfers between devices with their start and end apart: 10, of which 7 were waited for; matrix products, arithmetic and copies ran while one was open for 7% of the time, Pallas kernels for 0%

profile of v1, /device:TPU:1, one launch (start us, length us, event | category | flops | bytes accessed | tf_op | source)
XLA Modules:
  0.0 646.8 jit_solution(9161280172609846253)
XLA Ops:
  7.2 3.2 stack.2
  10.4 8.5 %all-to-all-start = ((bf16[8,4,4,8,1536]{4,3,2,1,0:T(8,128)(2,1)}), bf16[8,4,4,8,1536]{4,3,2,1,0:T(8,128)(2,1)}, u32[]{:S(2)}, u32[]{:S(2)}) async-start(bf16[8,4,4,8,1536]{4,3,2,1,0:T(8,128)(2,1)} %stack.2), calls=%async_computation | async-start | bytes 6291456 | tf_op jit(solution)/shard_map/all_to_all | solution.py:96
  19.5 61.5 %all_gather.15 = bf16[4,40,1536]{2,0,1:T(4,128)(2,1)S(1)} all-gather(bf16[4,5,1536]{2,0,1:T(4,128)(2,1)S(1)} %copy-done.5), channel_id=1, replica_groups=mesh['req'=4,'head'=8,'blk'=4] {'head'}, dimensions={1}, use_global_device_ids=true | all-gather | bytes 552960 | tf_op jit(solution)/shard_map/all_gather | solution.py:98
  86.1 2.4 bitcast_reduce_fusion
  88.7 2.9 fusion.10
  91.7 2.9 fusion.8
  94.7 2.0 fusion.23
  99.0 3.1 copy.97
  104.8 1.7 convert_element_type.142
  106.5 1.6 copy.100
  109.0 1.9 slice.285
  111.0 2.1 copy.99
  113.0 3.0 pad_maximum_fusion
  120.4 27.2 %all-gather.4.cloned.1.call-done = bf16[4,1184,3,64]{3,0,2,1:T(4,128)(2,1)} async-done(((bf16[4,296,3,64]{3,0,2,1:T(4,128)(2,1)}), bf16[4,1184,3,64]{3,0,2,1:T(4,128)(2,1)}) %all-gather.4.cloned.1.call-update) | async-done | bytes 1818640 | tf_op jit(solution)/shard_map/all_gather | solution.py:115
  147.6 10.5 %fusion = (f32[4,3,296]{2,1,0:T(4,128)S(1)}, f32[4,3,296,1184]{3,2,1,0:T(8,128)}) fusion(f32[4,1184]{1,0:T(4,128)S(1)} %or_convert_fusion, bf16[4,1184,3,64]{3,0,2,1:T(4,128)(2,1)} %all-gather.4.cloned.1.call-done, bf16[4,40,3,64]{1,3,2,0:T(8,128)(2,1)S(1)} %multiply_convert_fusion.3, bf16[4,256,3,64]{1,3,2,0:T(8,128)(2,1)} %multiply_convert_fusion.1), kind=kOutput, calls=%fused_computation.2 | convolution fusion | flops 551835136 | bytes 19128704 | tf_op jit(solution)/shard_map/rqhd,rkhd->rhqk/dot_general | solution.py:126
  158.1 34.0 %all-gather.6.cloned.1.call-done = bf16[4,1184,3,64]{3,0,2,1:T(4,128)(2,1)} async-done(((bf16[4,296,3,64]{3,0,2,1:T(4,128)(2,1)}), bf16[4,1184,3,64]{3,0,2,1:T(4,128)(2,1)}) %all-gather.6.cloned.1.call-update) | async-done | bytes 1818640 | tf_op jit(solution)/shard_map/all_gather | solution.py:116
  192.1 9.1 %divide_convert_fusion = bf16[4,296,3,64]{1,3,2,0:T(8,128)(2,1)S(1)} fusion(bf16[4,1184,3,64]{3,0,2,1:T(4,128)(2,1)} %all-gather.6.cloned.1.call-done, f32[4,3,296,1184]{3,2,1,0:T(8,128)} %get-tuple-element.49, f32[4,1184]{1,0:T(4,128)S(1)} %or_convert_fusion, f32[4,296,3]{1,2,0:T(4,128)S(1)} %bitcast.226), kind=kOutput, calls=%fused_computation.56 | convolution fusion | flops 547178496 | bytes 19128704 | tf_op jit(solution)/shard_map/rhqk,rkhd->rhqd/dot_general | solution.py:131
  201.2 2.7 fusion.14
  206.7 164.2 %all-reduce.11.cloned.1.call-done = (bf16[4,32,8,1536]{3,2,1,0:T(8,128)(2,1)}, bf16[4,40,1536]{2,0,1:T(4,128)(2,1)}) async-done(((bf16[4,32,8,1536]{3,2,1,0:T(8,128)(2,1)}, bf16[4,40,1536]{2,0,1:T(4,128)(2,1)}), (bf16[4,32,8,1536]{3,2,1,0:T(8,128)(2,1)}, bf16[4,40,1536]{2,0,1:T(4,128)(2,1)})) %all-reduce.11.cloned.1.call-update) | async-done | bytes 3637264
  373.5 2.1 add_convert_fusion.1
  379.3 30.7 %all_gather.19 = bf16[4,40,1536]{2,0,1:T(4,128)(2,1)S(1)} all-gather(bf16[4,5,1536]{2,0,1:T(4,128)(2,1)S(1)} %add_convert_fusion.5), channel_id=1, replica_groups=mesh['req'=4,'head'=8,'blk'=4] {'head'}, dimensions={1}, use_global_device_ids=true | all-gather | bytes 552960 | tf_op jit(solution)/shard_map/all_gather | solution.py:164
  410.0 4.8 convolution_convert_fusion.2
  414.8 2.1 copy.107
  416.8 23.0 %all-gather.8.cloned.1.call-done = bf16[4,32,8,1536]{3,2,1,0:T(8,128)(2,1)} async-done(((bf16[4,4,8,1536]{3,2,1,0:T(8,128)(2,1)}), bf16[4,32,8,1536]{3,2,1,0:T(8,128)(2,1)}) %all-gather.8.cloned.1.call-update) | async-done | bytes 3145744 | tf_op jit(solution)/shard_map/all_gather | solution.py:163
  439.8 10.5 %fusion.13 = bf16[4,32,8,1536]{3,2,1,0:T(8,128)(2,1)} fusion(bf16[768,1536]{1,0:T(8,128)(2,1)S(1)} %copy-done, bf16[1536,768]{1,0:T(8,128)(2,1)} %param.34, bf16[4,32,8,1536]{3,2,1,0:T(8,128)(2,1)} %all-gather.8.cloned.1.call-done), kind=kOutput, calls=%fused_computation.20 | convolution fusion | flops 4840488960 | bytes 11010048 | tf_op jit(solution)/shard_map/rnf,fd->rnd/dot_general | solution.py:175
  451.2 161.8 %all-reduce.9.cloned.1.call-done = (bf16[4,32,8,1536]{3,2,1,0:T(8,128)(2,1)}, bf16[4,40,1536]{2,0,1:T(4,128)(2,1)}) async-done(((bf16[4,32,8,1536]{3,2,1,0:T(8,128)(2,1)}, bf16[4,40,1536]{2,0,1:T(4,128)(2,1)}), (bf16[4,32,8,1536]{3,2,1,0:T(8,128)(2,1)}, bf16[4,40,1536]{2,0,1:T(4,128)(2,1)})) %all-reduce.9.cloned.1.call-update) | async-done | bytes 3637264
  614.4 2.2 multiply_reduce_fusion
  619.4 2.0 collective-permute-start
  624.5 2.8 collective-permute-done.1
  627.4 5.1 collective-permute-start.2
  632.5 1.9 collective-permute-start.3
  635.0 2.6 collective-permute-done.3
  (154 shorter events, 35.2 us)
Async XLA Ops:
  7.2 432.7 %copy-start = (bf16[768,1536]{1,0:T(8,128)(2,1)S(1)}, bf16[768,1536]{1,0:T(8,128)(2,1)}, u32[]{:S(2)}) copy-start(bf16[768,1536]{1,0:T(8,128)(2,1)} %param.36) | copy-start | bytes 7077892
  10.4 8.5 %copy-start.13 = (f32[4,6,1536]{2,0,1:T(4,128)S(1)}, f32[4,6,1536]{2,0,1:T(4,128)}, u32[]{:S(2)}) copy-start(f32[4,6,1536]{2,0,1:T(4,128)} %param.25) | copy-start | bytes 442372
  10.4 9.2 %copy-start.5 = (bf16[4,5,1536]{2,0,1:T(4,128)(2,1)S(1)}, bf16[4,5,1536]{2,0,1:T(4,128)(2,1)}, u32[]{:S(2)}) copy-start(bf16[4,5,1536]{2,0,1:T(4,128)(2,1)} %param.21) | copy-start | bytes 184324
  10.4 70.7 %copy-start.14 = (f32[4,6,1536]{2,0,1:T(4,128)S(1)}, f32[4,6,1536]{2,0,1:T(4,128)}, u32[]{:S(2)}) copy-start(f32[4,6,1536]{2,0,1:T(4,128)} %param.26) | copy-start | bytes 442372
  10.4 75.7 %all-to-all-start = ((bf16[8,4,4,8,1536]{4,3,2,1,0:T(8,128)(2,1)}), bf16[8,4,4,8,1536]{4,3,2,1,0:T(8,128)(2,1)}, u32[]{:S(2)}, u32[]{:S(2)}) async-start(bf16[8,4,4,8,1536]{4,3,2,1,0:T(8,128)(2,1)} %stack.2), calls=%async_computation | async-start | bytes 6291456 | tf_op jit(solution)/shard_map/all_to_all | solution.py:96
  18.8 128.8 %all-gather.4.cloned.1.call-start = ((), (), s32[]{:S(2)}) async-start(), calls=%async_computation.1 | async-start | bytes 4546560 | tf_op jit(solution)/shard_map/all_gather | solution.py:115
  18.9 64.8 %copy-start.2 = (bf16[1536,3,192]{0,2,1:T(8,128)(2,1)S(1)}, bf16[1536,3,192]{0,2,1:T(8,128)(2,1)}, u32[]{:S(2)}) copy-start(bf16[1536,3,192]{0,2,1:T(8,128)(2,1)} %param.31) | copy-start | bytes 5308420
  83.2 2.8 copy-start.23
  83.2 2.8 copy-start.24
  86.1 5.6 copy-start.15
  86.1 5.6 copy-start.16
  91.7 2.9 copy-start.26
  102.2 89.9 %all-gather.6.cloned.1.call-start = ((), (), s32[]{:S(2)}) async-start(), calls=%async_computation.2 | async-start | bytes 4546560 | tf_op jit(solution)/shard_map/all_gather | solution.py:116
  108.4 11.0 %copy-start.25 = (s32[4]{0:T(128)S(1)}, s32[4]{0:T(128)}, u32[]{:S(2)}) copy-start(s32[4]{0:T(128)} %param.23) | copy-start | bytes 52
  116.0 254.9 %all-reduce.11.cloned.1.call-start = ((), (), s32[]{:S(2)}) async-start(), calls=%async_computation.5 | async-start | bytes 7274496
  192.1 9.1 %copy-start.9 = (bf16[192,1536]{1,0:T(8,128)(2,1)S(1)}, bf16[192,1536]{1,0:T(8,128)(2,1)}, u32[]{:S(2)}) copy-start(bf16[192,1536]{1,0:T(8,128)(2,1)} %param.32) | copy-start | bytes 1769476
  203.9 167.0 %copy-start.1 = (bf16[4,4,8,1536]{3,2,1,0:T(8,128)(2,1)S(1)}, bf16[4,4,8,1536]{3,2,1,0:T(8,128)(2,1)}, u32[]{:S(2)}) copy-start(bf16[4,4,8,1536]{3,2,1,0:T(8,128)(2,1)} %param.20) | copy-start | bytes 1179652
  203.9 167.0 %copy-start.6 = (f32[4,1536]{1,0:T(4,128)S(1)}, f32[4,1536]{1,0:T(4,128)}, u32[]{:S(2)}) copy-start(f32[4,1536]{1,0:T(4,128)} %get-tuple-element.38) | copy-start | bytes 73732
  204.3 169.2 %copy-start.21 = (f32[4,1536]{1,0:T(4,128)S(1)}, f32[4,1536]{1,0:T(4,128)}, u32[]{:S(2)}) copy-start(f32[4,1536]{1,0:T(4,128)} %get-tuple-element.39) | copy-start | bytes 73732
  205.3 170.9 %copy-start.19 = (f32[4,1,1536]{2,0,1:T(4,128)S(1)}, f32[4,1,1536]{2,0,1:T(4,128)}, u32[]{:S(2)}) copy-start(f32[4,1,1536]{2,0,1:T(4,128)} %get-tuple-element.32) | copy-start | bytes 73732
  205.3 171.0 %copy-start.7 = (f32[4,1536]{1,0:T(4,128)S(1)}, f32[4,1536]{1,0:T(4,128)}, u32[]{:S(2)}) copy-start(f32[4,1536]{1,0:T(4,128)} %get-tuple-element.30) | copy-start | bytes 73732
  205.3 173.0 %copy-start.18 = (f32[4,1536]{1,0:T(4,128)S(1)}, f32[4,1536]{1,0:T(4,128)}, u32[]{:S(2)}) copy-start(f32[4,1536]{1,0:T(4,128)} %get-tuple-element.33) | copy-start | bytes 73732
  205.4 234.5 %all-gather.8.cloned.1.call-start = ((), (), s32[]{:S(2)}) async-start(), calls=%async_computation.3 | async-start | bytes 3538944 | tf_op jit(solution)/shard_map/all_gather | solution.py:163
  375.6 237.4 %all-reduce.9.cloned.1.call-start = ((), (), s32[]{:S(2)}) async-start(), calls=%async_computation.4 | async-start | bytes 7274496
  450.3 162.7 %copy-start.11 = (f32[4,1536]{1,0:T(4,128)S(1)}, f32[4,1536]{1,0:T(4,128)}, u32[]{:S(2)}) copy-start(f32[4,1536]{1,0:T(4,128)} %get-tuple-element.34) | copy-start | bytes 73732
  451.1 167.4 %copy-start.10 = (f32[4,8,16,16]{3,2,1,0:T(8,128)S(1)}, f32[4,8,16,16]{3,2,1,0:T(8,128)}, u32[]{:S(2)}) copy-start(f32[4,8,16,16]{3,2,1,0:T(8,128)} %param.22) | copy-start | bytes 98308
  614.4 8.3 %copy-start.17 = (f32[4,1536]{1,0:T(4,128)S(1)}, f32[4,1536]{1,0:T(4,128)}, u32[]{:S(2)}) copy-start(f32[4,1536]{1,0:T(4,128)} %get-tuple-element.28) | copy-start | bytes 73732
  614.4 9.9 %copy-start.12 = (bf16[3,3,16,512]{3,2,1,0:T(8,128)(2,1)S(1)}, bf16[3,3,16,512]{3,2,1,0:T(8,128)(2,1)}, u32[]{:S(2)}) copy-start(bf16[3,3,16,512]{3,2,1,0:T(8,128)(2,1)} %param.39) | copy-start | bytes 442372
  619.4 5.1 collective-permute-start
  621.4 6.0 collective-permute-start.1
  627.4 7.6 %collective-permute-start.2 = (bf16[4,10,1,16]{3,2,1,0:T(2,128)(2,1)S(1)}, bf16[4,10,1,16]{3,2,1,0:T(2,128)(2,1)S(1)}, u32[]{:S(2)}, u32[]{:S(2)}) collective-permute-start(bf16[4,10,1,16]{3,2,1,0:T(2,128)(2,1)S(1)} %get-tuple-element.26), channel_id=1, source_target_pairs={{0,1},{1,2},{2,3},{4,5},{5,6},{6,7},{8,9},{9,10},{10,11},{12,13},{... | collective-permute-start | bytes 3848 | tf_op jit(solution)/shard_map/ppermute | solution.py:15
  632.5 5.1 collective-permute-start.3
  (7 other events, 9.5 us)
Sparse Core Ops, SparseCore 0:
  102.3 45.3 all-gather.3
  149.3 42.7 all-gather.5
  205.5 165.4 all-reduce.10
  375.7 64.0 all-gather.7
  450.4 162.4 all-reduce.8
